TPU v7x, 128 devices: a whole 4x4x4 slice. The times are simulated.
128 devices in a mesh: seq: 16 (over y, x), emb: 8 (over z, core).
Axes of the slice: x: 4, y: 4, z: 4, core: 2. Of those that a mesh axis runs over, the one named last changes fastest.
Arguments:
- source: bfloat16 [32768, 1024], P('seq', 'emb'), may hold values from -6 to 6
- target: bfloat16 [32768, 1024], P('seq', 'emb'), may hold values from -6 to 6
- doc_ids: int32 [32768], replicated, may hold values from 0 to 511, never falling along the last dimension, each value on 1 to 512 neighbouring positions
- offsets: int32 [512], P(('seq', 'emb')), may hold values from -2048 to 2048, as said below
Outputs:
- projected: bfloat16 [32768, 1024], P('seq', 'emb')
- row_mass: float32 [32768], P(('seq', 'emb'))
Inputs may be any that keep to these rules, and one draw needn't show every extreme that they name: doc_ids never fall along the sentences. `offsets`: both ends of the range occur in every draw.
All inputs are finite; a program needn't handle non-finite values.
Results may differ from a plain program's by a relative error of at most 0.006.
Values may be sent and summed in bfloat16 or wider, within the bound.
No kernel may reach another device: no remote copies, remote signals or barrier semaphores. Data moves between devices by JAX's collectives and lax.ppermute only.
A program may use at most 128 MiB of HBM per device.

v0:
```python
import jax
import jax.numpy as jnp
from jax import lax
from jax.sharding import PartitionSpec as P

BAND = 2048
OFFSET_BLOCK = 64
ITERS = 3
INV_EPS = 50.0
PENALTY = 0.04


def shifted_2(block, axis, distance):
    devices = range(lax.axis_size(axis))
    route = [(i - distance, i) for i in devices if i - distance in devices]
    return lax.ppermute(block, axis, route)


def per_device(source, target, doc_ids, offsets):
    n_emb = lax.axis_size("emb")
    rows_dev = source.shape[0] // n_emb
    place = lax.axis_index(("seq", "emb"))
    sentences = doc_ids.shape[0]
    reach = 2 * BAND
    hops = reach // rows_dev
    width = rows_dev + 2 * reach
    src_rows, tgt_rows = (
        lax.all_to_all(source, "emb", split_axis=0, concat_axis=1, tiled=True),
        lax.all_to_all(target, "emb", split_axis=0, concat_axis=1, tiled=True),
    )
    lower = {}
    upper = {}
    for dist in range(1, hops + 1):
        for sign in (1, -1):
            moved = shifted_2(tgt_rows, ("seq", "emb"), -sign * dist)
            if sign > 0:
                upper[dist] = moved
            else:
                lower[dist] = moved
    pieces = (
        [lower[dist] for dist in range(hops, 0, -1)]
        + [tgt_rows]
        + [upper[dist] for dist in range(1, hops + 1)]
    )
    window = jnp.concatenate(pieces, axis=0)
    src_scale = lax.rsqrt(jnp.sum(jnp.square(src_rows.astype(jnp.float32)), axis=1) + 1e-06)
    tgt_scale = lax.rsqrt(jnp.sum(jnp.square(window.astype(jnp.float32)), axis=1) + 1e-06)
    first_row = place * rows_dev
    src_pos = first_row + jnp.arange(rows_dev, dtype=jnp.int32)
    tgt_pos = first_row - reach + jnp.arange(width, dtype=jnp.int32)
    valid = (tgt_pos >= 0) & (tgt_pos < sentences)
    shifted = jnp.repeat(offsets, OFFSET_BLOCK)
    band = (jnp.abs(tgt_pos[None, :] - src_pos[:, None] - shifted[:, None]) <= BAND) & valid[
        None, :
    ]
    pad_docs = jnp.pad(doc_ids, (reach, reach), constant_values=-1)
    same = (
        lax.dynamic_slice_in_dim(doc_ids, first_row, rows_dev, 0)[:, None]
        == lax.dynamic_slice_in_dim(pad_docs, first_row, width, 0)[None, :]
    )
    penalty = jnp.where(same, 0.0, PENALTY)

    def cosines():
        dots = lax.dot_general(
            src_rows, window, (((1,), (1,)), ((), ())), preferred_element_type=jnp.float32
        )
        return dots * src_scale[:, None] * tgt_scale[None, :]

    def to_kernel(cosine):
        return jnp.where(band, jnp.exp((cosine - penalty) * INV_EPS), 0.0)

    def kernel():
        return to_kernel(cosines())

    padded_len = sentences + 2 * reach

    def column_scaling(part):
        full = lax.dynamic_update_slice_in_dim(
            jnp.zeros((padded_len,), jnp.float32), part, first_row, 0
        )
        columns = lax.psum(full, ("seq", "emb"))
        mine = lax.dynamic_slice_in_dim(columns, first_row, width, 0)
        return jnp.where(valid, 1.0 / jnp.where(valid, mine, 1.0), 0.0)

    scaling = valid.astype(jnp.float32)
    inverse = jnp.zeros((rows_dev,), jnp.float32)
    for step in range(ITERS):
        kern = kernel()
        inverse = 1.0 / jnp.sum(kern * scaling[None, :], axis=1)
        part = jnp.sum(kern * inverse[:, None], axis=0)
        scaling = column_scaling(part)
    kern = kernel()
    totals = jnp.sum(kern * scaling[None, :], axis=1)
    row_mass = inverse * totals
    weights = (kern * scaling[None, :] / totals[:, None]).astype(jnp.bfloat16)
    mixed = jnp.dot(weights, window, preferred_element_type=jnp.float32).astype(jnp.bfloat16)
    projected = lax.all_to_all(mixed, "emb", split_axis=1, concat_axis=0, tiled=True)
    return (projected, row_mass)


def solution(mesh):
    in_specs = (P("seq", "emb"), P("seq", "emb"), P(), P(("seq", "emb")))
    out_specs = (P("seq", "emb"), P(("seq", "emb")))
    return jax.shard_map(
        per_device, mesh=mesh, in_specs=in_specs, out_specs=out_specs, check_vma=False
    )
```

profile of v0, /device:TPU:1, one launch (start us, length us, event | category | flops | bytes accessed | tf_op | source)
XLA Modules:
  0.0 916.7 jit_solution(1106504656335570832)
XLA Ops:
  7.2 6.8 all-to-all-start
  14.0 9.3 %all-to-all-done = bf16[8,256,128]{2,1,0:T(8,128)(2,1)S(1)} async-done(((bf16[8,256,128]{2,1,0:T(8,128)(2,1)}), bf16[8,256,128]{2,1,0:T(8,128)(2,1)S(1)}, u32[]{:S(2)}, u32[]{:S(2)}) %all-to-all-start) | async-done | bytes 524320 | tf_op jit(solution)/shard_map/all_to_all | solution.py:29
  23.3 4.4 all-to-all-start.1
  28.7 5.5 collective-permute-start
  38.6 6.4 collective-permute-start.2
  48.3 4.7 collective-permute-start.4
  53.4 6.1 collective-permute-start.5
  62.5 4.5 collective-permute-done.2
  67.1 5.0 collective-permute-start.7
  73.2 5.1 collective-permute-done.3
  79.6 9.9 %collective-permute-done.4 = bf16[256,1024]{0,1:T(8,128)(2,1)S(1)} collective-permute-done((bf16[256,1024]{0,1:T(8,128)(2,1)S(1)}, bf16[256,1024]{0,1:T(8,128)(2,1)S(1)}, u32[]{:S(2)}, u32[]{:S(2)}) %collective-permute-start.4) | collective-permute-done | bytes 524320 | tf_op jit(solution)/shard_map/ppermute | solution.py:16
  89.5 11.1 %collective-permute-start.9 = (bf16[256,1024]{0,1:T(8,128)(2,1)S(1)}, bf16[256,1024]{0,1:T(8,128)(2,1)S(1)}, u32[]{:S(2)}, u32[]{:S(2)}) collective-permute-start(bf16[256,1024]{0,1:T(8,128)(2,1)S(1)} %bitcast.38), channel_id=1, source_target_pairs={{0,7},{1,8},{2,9},{3,10},{4,11},{5,12},{6,13},{7,14},{8,15},{9,16}... | collective-permute-start | bytes 1572872 | tf_op jit(solution)/shard_map/ppermute | solution.py:16
  100.8 4.3 collective-permute-start.10
  105.1 6.9 collective-permute-done.6
  112.0 6.5 collective-permute-start.11
  118.5 4.7 collective-permute-done.7
  123.2 4.6 collective-permute-start.12
  127.9 6.6 collective-permute-done.8
  134.5 6.6 collective-permute-start.13
  141.1 7.7 collective-permute-start.14
  148.8 13.2 %collective-permute-start.15 = (bf16[256,1024]{0,1:T(8,128)(2,1)S(1)}, bf16[256,1024]{0,1:T(8,128)(2,1)S(1)}, u32[]{:S(2)}, u32[]{:S(2)}) collective-permute-start(bf16[256,1024]{0,1:T(8,128)(2,1)S(1)} %bitcast.44), channel_id=1, source_target_pairs={{0,1},{1,2},{2,3},{3,4},{4,5},{5,6},{6,7},{7,8},{8,9},{9,10},{10,1... | collective-permute-start | bytes 1572872 | tf_op jit(solution)/shard_map/ppermute | solution.py:16
  169.5 6.2 collective-permute-done.16
  177.0 3.9 collective-permute-done.17
  182.3 12.5 %collective-permute-done.18 = bf16[256,1024]{0,1:T(8,128)(2,1)S(1)} collective-permute-done((bf16[256,1024]{0,1:T(8,128)(2,1)S(1)}, bf16[256,1024]{0,1:T(8,128)(2,1)S(1)}, u32[]{:S(2)}, u32[]{:S(2)}) %collective-permute-start.18) | collective-permute-done | bytes 524320 | tf_op jit(solution)/shard_map/ppermute | solution.py:16
  196.2 9.9 %collective-permute-done.19 = bf16[256,1024]{0,1:T(8,128)(2,1)S(1)} collective-permute-done((bf16[256,1024]{0,1:T(8,128)(2,1)S(1)}, bf16[256,1024]{0,1:T(8,128)(2,1)S(1)}, u32[]{:S(2)}, u32[]{:S(2)}) %collective-permute-start.19) | collective-permute-done | bytes 524320 | tf_op jit(solution)/shard_map/ppermute | solution.py:16
  207.4 14.2 %collective-permute-done.20 = bf16[256,1024]{0,1:T(8,128)(2,1)S(1)} collective-permute-done((bf16[256,1024]{0,1:T(8,128)(2,1)S(1)}, bf16[256,1024]{0,1:T(8,128)(2,1)S(1)}, u32[]{:S(2)}, u32[]{:S(2)}) %collective-permute-start.20) | collective-permute-done | bytes 524320 | tf_op jit(solution)/shard_map/ppermute | solution.py:16
  222.9 9.9 %collective-permute-done.21 = bf16[256,1024]{0,1:T(8,128)(2,1)S(1)} collective-permute-done((bf16[256,1024]{0,1:T(8,128)(2,1)S(1)}, bf16[256,1024]{0,1:T(8,128)(2,1)S(1)}, u32[]{:S(2)}, u32[]{:S(2)}) %collective-permute-start.21) | collective-permute-done | bytes 524320 | tf_op jit(solution)/shard_map/ppermute | solution.py:16
  234.1 28.2 %collective-permute-done.22 = bf16[256,1024]{0,1:T(8,128)(2,1)S(1)} collective-permute-done((bf16[256,1024]{0,1:T(8,128)(2,1)S(1)}, bf16[256,1024]{0,1:T(8,128)(2,1)S(1)}, u32[]{:S(2)}, u32[]{:S(2)}) %collective-permute-start.22) | collective-permute-done | bytes 524320 | tf_op jit(solution)/shard_map/ppermute | solution.py:16
  266.6 26.9 %collective-permute-done.24 = bf16[256,1024]{0,1:T(8,128)(2,1)S(1)} collective-permute-done((bf16[256,1024]{0,1:T(8,128)(2,1)S(1)}, bf16[256,1024]{0,1:T(8,128)(2,1)S(1)}, u32[]{:S(2)}, u32[]{:S(2)}) %collective-permute-start.24) | collective-permute-done | bytes 524320 | tf_op jit(solution)/shard_map/ppermute | solution.py:16
  294.9 4.1 collective-permute-done.25
  300.3 8.9 collective-permute-done.26
  310.6 15.1 %collective-permute-done.27 = bf16[256,1024]{0,1:T(8,128)(2,1)S(1)} collective-permute-done((bf16[256,1024]{0,1:T(8,128)(2,1)S(1)}, bf16[256,1024]{0,1:T(8,128)(2,1)S(1)}, u32[]{:S(2)}, u32[]{:S(2)}) %collective-permute-start.27) | collective-permute-done | bytes 524320 | tf_op jit(solution)/shard_map/ppermute | solution.py:16
  325.7 8.9 collective-permute-done.28
  334.7 4.0 collective-permute-done.29
  338.7 35.5 %collective-permute-done.30 = bf16[256,1024]{0,1:T(8,128)(2,1)S(1)} collective-permute-done((bf16[256,1024]{0,1:T(8,128)(2,1)S(1)}, bf16[256,1024]{0,1:T(8,128)(2,1)S(1)}, u32[]{:S(2)}, u32[]{:S(2)}) %collective-permute-start.30) | collective-permute-done | bytes 524320 | tf_op jit(solution)/shard_map/ppermute | solution.py:16
  374.7 4.0 multiply_reduce_fusion
  378.6 11.5 %multiply_reduce_fusion.6 = (f32[256]{0:T(256)S(1)}, f32[256,8448]{0,1:T(8,128)S(1)}) fusion(f32[8448]{0:T(1024)S(1)} %get-tuple-element.5, s32[8448]{0:T(1024)S(1)} %get-tuple-element.6, s32[256]{0:T(256)S(1)} %dynamic_slice.15, f32[8448]{0:T(1024)S(1)} %add_rsqrt_fusion, f32[256]{0:T(256)S(1)} %add_rsqrt_fusion.1, ...), kind=kOutput, calls=%fused_computation.14 | convolution fusion | flops 4459462656 | bytes 26625280 | tf_op jit(solution)/shard_map/dot_general | solution.py:64
  396.2 171.8 %all-reduce.5.cloned.1.call-done = f32[40960]{0:T(1024)} async-done(((f32[40960]{0:T(1024)}), f32[40960]{0:T(1024)}) %all-reduce.5.cloned.1.call-update) | async-done | bytes 163856 | tf_op jit(solution)/shard_map/psum | solution.py:81
  568.9 5.7 multiply_reduce_fusion.4
  574.6 4.2 multiply_reduce_fusion.3
  580.2 141.7 %all-reduce.7.cloned.1.call-done = f32[40960]{0:T(1024)} async-done(((f32[40960]{0:T(1024)}), f32[40960]{0:T(1024)}) %all-reduce.7.cloned.1.call-update) | async-done | bytes 163856 | tf_op jit(solution)/shard_map/psum | solution.py:81
  722.8 5.7 multiply_reduce_fusion.2
  728.5 4.2 multiply_reduce_fusion.1
  734.0 141.8 %all-reduce.9.cloned.1.call-done = f32[40960]{0:T(1024)} async-done(((f32[40960]{0:T(1024)}), f32[40960]{0:T(1024)}) %all-reduce.9.cloned.1.call-update) | async-done | bytes 163856 | tf_op jit(solution)/shard_map/psum | solution.py:81
  876.7 5.7 multiply_reduce_fusion.7
  882.4 12.8 %fusion.11 = bf16[32,8,8,128]{3,2,1,0:T(8,128)(2,1)S(1)} fusion(bf16[8448,1024]{0,1:T(8,128)(2,1)} %copy-done.1, f32[256,8448]{0,1:T(8,128)} %copy-done, f32[256]{0:T(256)S(1)} %multiply_reduce_fusion.7, f32[8448]{0:T(1024)S(1)} %divide_select_fusion), kind=kOutput, calls=%fused_computation.22 | convolution fusion | flops 4435935232 | bytes 26511360 | tf_op jit(solution)/shard_map/dot_general | solution.py:96
  896.1 3.9 all-to-all-start.2
  900.6 8.8 all-to-all-done.2
  (109 shorter events, 52.4 us)
Async XLA Ops:
  7.2 16.2 %all-to-all-start = ((bf16[8,256,128]{2,1,0:T(8,128)(2,1)}), bf16[8,256,128]{2,1,0:T(8,128)(2,1)S(1)}, u32[]{:S(2)}, u32[]{:S(2)}) async-start(bf16[8,256,128]{2,1,0:T(8,128)(2,1)} %bitcast.64), calls=%async_computation | async-start | bytes 1048576 | tf_op jit(solution)/shard_map/all_to_all | solution.py:29
  23.3 29.6 %all-to-all-start.1 = ((bf16[8,256,128]{2,1,0:T(8,128)(2,1)}), bf16[8,256,128]{2,1,0:T(8,128)(2,1)S(1)}, u32[]{:S(2)}, u32[]{:S(2)}) async-start(bf16[8,256,128]{2,1,0:T(8,128)(2,1)} %bitcast.65), calls=%async_computation.1 | async-start | bytes 1048576 | tf_op jit(solution)/shard_map/all_to_all | solution.py:28
  27.7 540.3 %all-reduce.5.cloned.1.call-start = ((), (), s32[]{:S(2)}) async-start(), calls=%async_computation.3 | async-start | bytes 327680 | tf_op jit(solution)/shard_map/psum | solution.py:81
  28.7 24.6 %collective-permute-start = (bf16[256,1024]{0,1:T(8,128)(2,1)S(1)}, bf16[256,1024]{0,1:T(8,128)(2,1)}, u32[]{:S(2)}, u32[]{:S(2)}) collective-permute-start(bf16[256,1024]{0,1:T(8,128)(2,1)S(1)} %bitcast.29), channel_id=1, source_target_pairs={{0,16},{1,17},{2,18},{3,19},{4,20},{5,21},{6,22},{7,23},{8,24},{9,... | collective-permute-start | bytes 1572872 | tf_op jit(solution)/shard_map/ppermute | solution.py:16
  34.3 26.3 %collective-permute-start.1 = (bf16[256,1024]{0,1:T(8,128)(2,1)S(1)}, bf16[256,1024]{0,1:T(8,128)(2,1)S(1)}, u32[]{:S(2)}, u32[]{:S(2)}) collective-permute-start(bf16[256,1024]{0,1:T(8,128)(2,1)S(1)} %bitcast.30), channel_id=1, source_target_pairs={{0,15},{1,16},{2,17},{3,18},{4,19},{5,20},{6,21},{7,22},{8,23},{9,... | collective-permute-start | bytes 1572872 | tf_op jit(solution)/shard_map/ppermute | solution.py:16
  38.6 28.5 %collective-permute-start.2 = (bf16[256,1024]{0,1:T(8,128)(2,1)S(1)}, bf16[256,1024]{0,1:T(8,128)(2,1)}, u32[]{:S(2)}, u32[]{:S(2)}) collective-permute-start(bf16[256,1024]{0,1:T(8,128)(2,1)S(1)} %bitcast.31), channel_id=1, source_target_pairs={{0,14},{1,15},{2,16},{3,17},{4,18},{5,19},{6,20},{7,21},{8,22},{9,... | collective-permute-start | bytes 1572872 | tf_op jit(solution)/shard_map/ppermute | solution.py:16
  45.0 33.3 %collective-permute-start.3 = (bf16[256,1024]{0,1:T(8,128)(2,1)S(1)}, bf16[256,1024]{0,1:T(8,128)(2,1)S(1)}, u32[]{:S(2)}, u32[]{:S(2)}) collective-permute-start(bf16[256,1024]{0,1:T(8,128)(2,1)S(1)} %bitcast.32), channel_id=1, source_target_pairs={{0,13},{1,14},{2,15},{3,16},{4,17},{5,18},{6,19},{7,20},{8,21},{9,... | collective-permute-start | bytes 1572872 | tf_op jit(solution)/shard_map/ppermute | solution.py:16
  48.3 41.3 %collective-permute-start.4 = (bf16[256,1024]{0,1:T(8,128)(2,1)S(1)}, bf16[256,1024]{0,1:T(8,128)(2,1)S(1)}, u32[]{:S(2)}, u32[]{:S(2)}) collective-permute-start(bf16[256,1024]{0,1:T(8,128)(2,1)S(1)} %bitcast.33), channel_id=1, source_target_pairs={{0,12},{1,13},{2,14},{3,15},{4,16},{5,17},{6,18},{7,19},{8,20},{9,... | collective-permute-start | bytes 1572872 | tf_op jit(solution)/shard_map/ppermute | solution.py:16
  53.4 47.4 %collective-permute-start.5 = (bf16[256,1024]{0,1:T(8,128)(2,1)S(1)}, bf16[256,1024]{0,1:T(8,128)(2,1)S(1)}, u32[]{:S(2)}, u32[]{:S(2)}) collective-permute-start(bf16[256,1024]{0,1:T(8,128)(2,1)S(1)} %bitcast.34), channel_id=1, source_target_pairs={{0,11},{1,12},{2,13},{3,14},{4,15},{5,16},{6,17},{7,18},{8,19},{9,... | collective-permute-start | bytes 1572872 | tf_op jit(solution)/shard_map/ppermute | solution.py:16
  60.5 51.5 %collective-permute-start.6 = (bf16[256,1024]{0,1:T(8,128)(2,1)S(1)}, bf16[256,1024]{0,1:T(8,128)(2,1)S(1)}, u32[]{:S(2)}, u32[]{:S(2)}) collective-permute-start(bf16[256,1024]{0,1:T(8,128)(2,1)S(1)} %bitcast.35), channel_id=1, source_target_pairs={{0,10},{1,11},{2,12},{3,13},{4,14},{5,15},{6,16},{7,17},{8,18},{9,... | collective-permute-start | bytes 1572872 | tf_op jit(solution)/shard_map/ppermute | solution.py:16
  67.1 56.2 %collective-permute-start.7 = (bf16[256,1024]{0,1:T(8,128)(2,1)S(1)}, bf16[256,1024]{0,1:T(8,128)(2,1)S(1)}, u32[]{:S(2)}, u32[]{:S(2)}) collective-permute-start(bf16[256,1024]{0,1:T(8,128)(2,1)S(1)} %bitcast.36), channel_id=1, source_target_pairs={{0,9},{1,10},{2,11},{3,12},{4,13},{5,14},{6,15},{7,16},{8,17},{9,1... | collective-permute-start | bytes 1572872 | tf_op jit(solution)/shard_map/ppermute | solution.py:16
  78.3 56.2 %collective-permute-start.8 = (bf16[256,1024]{0,1:T(8,128)(2,1)S(1)}, bf16[256,1024]{0,1:T(8,128)(2,1)S(1)}, u32[]{:S(2)}, u32[]{:S(2)}) collective-permute-start(bf16[256,1024]{0,1:T(8,128)(2,1)S(1)} %bitcast.37), channel_id=1, source_target_pairs={{0,8},{1,9},{2,10},{3,11},{4,12},{5,13},{6,14},{7,15},{8,16},{9,17... | collective-permute-start | bytes 1572872 | tf_op jit(solution)/shard_map/ppermute | solution.py:16
  89.5 51.6 %collective-permute-start.9 = (bf16[256,1024]{0,1:T(8,128)(2,1)S(1)}, bf16[256,1024]{0,1:T(8,128)(2,1)S(1)}, u32[]{:S(2)}, u32[]{:S(2)}) collective-permute-start(bf16[256,1024]{0,1:T(8,128)(2,1)S(1)} %bitcast.38), channel_id=1, source_target_pairs={{0,7},{1,8},{2,9},{3,10},{4,11},{5,12},{6,13},{7,14},{8,15},{9,16}... | collective-permute-start | bytes 1572872 | tf_op jit(solution)/shard_map/ppermute | solution.py:16
  100.8 48.1 %collective-permute-start.10 = (bf16[256,1024]{0,1:T(8,128)(2,1)S(1)}, bf16[256,1024]{0,1:T(8,128)(2,1)S(1)}, u32[]{:S(2)}, u32[]{:S(2)}) collective-permute-start(bf16[256,1024]{0,1:T(8,128)(2,1)S(1)} %bitcast.39), channel_id=1, source_target_pairs={{0,6},{1,7},{2,8},{3,9},{4,10},{5,11},{6,12},{7,13},{8,14},{9,15},... | collective-permute-start | bytes 1572872 | tf_op jit(solution)/shard_map/ppermute | solution.py:16
  112.0 50.1 %collective-permute-start.11 = (bf16[256,1024]{0,1:T(8,128)(2,1)S(1)}, bf16[256,1024]{0,1:T(8,128)(2,1)S(1)}, u32[]{:S(2)}, u32[]{:S(2)}) collective-permute-start(bf16[256,1024]{0,1:T(8,128)(2,1)S(1)} %bitcast.40), channel_id=1, source_target_pairs={{0,5},{1,6},{2,7},{3,8},{4,9},{5,10},{6,11},{7,12},{8,13},{9,14},{... | collective-permute-start | bytes 1572872 | tf_op jit(solution)/shard_map/ppermute | solution.py:16
  123.2 40.8 %collective-permute-start.12 = (bf16[256,1024]{0,1:T(8,128)(2,1)S(1)}, bf16[256,1024]{0,1:T(8,128)(2,1)S(1)}, u32[]{:S(2)}, u32[]{:S(2)}) collective-permute-start(bf16[256,1024]{0,1:T(8,128)(2,1)S(1)} %bitcast.41), channel_id=1, source_target_pairs={{0,4},{1,5},{2,6},{3,7},{4,8},{5,9},{6,10},{7,11},{8,12},{9,13},{1... | collective-permute-start | bytes 1572872 | tf_op jit(solution)/shard_map/ppermute | solution.py:16
  134.5 30.9 %collective-permute-start.13 = (bf16[256,1024]{0,1:T(8,128)(2,1)S(1)}, bf16[256,1024]{0,1:T(8,128)(2,1)S(1)}, u32[]{:S(2)}, u32[]{:S(2)}) collective-permute-start(bf16[256,1024]{0,1:T(8,128)(2,1)S(1)} %bitcast.42), channel_id=1, source_target_pairs={{0,3},{1,4},{2,5},{3,6},{4,7},{5,8},{6,9},{7,10},{8,11},{9,12},{10... | collective-permute-start | bytes 1572872 | tf_op jit(solution)/shard_map/ppermute | solution.py:16
  141.1 25.7 %collective-permute-start.14 = (bf16[256,1024]{0,1:T(8,128)(2,1)S(1)}, bf16[256,1024]{0,1:T(8,128)(2,1)S(1)}, u32[]{:S(2)}, u32[]{:S(2)}) collective-permute-start(bf16[256,1024]{0,1:T(8,128)(2,1)S(1)} %bitcast.43), channel_id=1, source_target_pairs={{0,2},{1,3},{2,4},{3,5},{4,6},{5,7},{6,8},{7,9},{8,10},{9,11},{10,... | collective-permute-start | bytes 1572872 | tf_op jit(solution)/shard_map/ppermute | solution.py:16
  148.8 19.3 %collective-permute-start.15 = (bf16[256,1024]{0,1:T(8,128)(2,1)S(1)}, bf16[256,1024]{0,1:T(8,128)(2,1)S(1)}, u32[]{:S(2)}, u32[]{:S(2)}) collective-permute-start(bf16[256,1024]{0,1:T(8,128)(2,1)S(1)} %bitcast.44), channel_id=1, source_target_pairs={{0,1},{1,2},{2,3},{3,4},{4,5},{5,6},{6,7},{7,8},{8,9},{9,10},{10,1... | collective-permute-start | bytes 1572872 | tf_op jit(solution)/shard_map/ppermute | solution.py:16
  162.1 13.6 %collective-permute-start.16 = (bf16[256,1024]{0,1:T(8,128)(2,1)S(1)}, bf16[256,1024]{0,1:T(8,128)(2,1)S(1)}, u32[]{:S(2)}, u32[]{:S(2)}) collective-permute-start(bf16[256,1024]{0,1:T(8,128)(2,1)S(1)} %bitcast.45), channel_id=1, source_target_pairs={{1,0},{2,1},{3,2},{4,3},{5,4},{6,5},{7,6},{8,7},{9,8},{10,9},{11,1... | collective-permute-start | bytes 1572872 | tf_op jit(solution)/shard_map/ppermute | solution.py:16
  164.0 16.9 %collective-permute-start.17 = (bf16[256,1024]{0,1:T(8,128)(2,1)S(1)}, bf16[256,1024]{0,1:T(8,128)(2,1)S(1)}, u32[]{:S(2)}, u32[]{:S(2)}) collective-permute-start(bf16[256,1024]{0,1:T(8,128)(2,1)S(1)} %bitcast.46), channel_id=1, source_target_pairs={{2,0},{3,1},{4,2},{5,3},{6,4},{7,5},{8,6},{9,7},{10,8},{11,9},{12,... | collective-permute-start | bytes 1572872 | tf_op jit(solution)/shard_map/ppermute | solution.py:16
  165.4 29.4 %collective-permute-start.18 = (bf16[256,1024]{0,1:T(8,128)(2,1)S(1)}, bf16[256,1024]{0,1:T(8,128)(2,1)S(1)}, u32[]{:S(2)}, u32[]{:S(2)}) collective-permute-start(bf16[256,1024]{0,1:T(8,128)(2,1)S(1)} %bitcast.47), channel_id=1, source_target_pairs={{3,0},{4,1},{5,2},{6,3},{7,4},{8,5},{9,6},{10,7},{11,8},{12,9},{13... | collective-permute-start | bytes 1572872 | tf_op jit(solution)/shard_map/ppermute | solution.py:16
  166.7 39.3 %collective-permute-start.19 = (bf16[256,1024]{0,1:T(8,128)(2,1)S(1)}, bf16[256,1024]{0,1:T(8,128)(2,1)S(1)}, u32[]{:S(2)}, u32[]{:S(2)}) collective-permute-start(bf16[256,1024]{0,1:T(8,128)(2,1)S(1)} %bitcast.48), channel_id=1, source_target_pairs={{4,0},{5,1},{6,2},{7,3},{8,4},{9,5},{10,6},{11,7},{12,8},{13,9},{1... | collective-permute-start | bytes 1572872 | tf_op jit(solution)/shard_map/ppermute | solution.py:16
  168.1 53.4 %collective-permute-start.20 = (bf16[256,1024]{0,1:T(8,128)(2,1)S(1)}, bf16[256,1024]{0,1:T(8,128)(2,1)S(1)}, u32[]{:S(2)}, u32[]{:S(2)}) collective-permute-start(bf16[256,1024]{0,1:T(8,128)(2,1)S(1)} %bitcast.49), channel_id=1, source_target_pairs={{5,0},{6,1},{7,2},{8,3},{9,4},{10,5},{11,6},{12,7},{13,8},{14,9},{... | collective-permute-start | bytes 1572872 | tf_op jit(solution)/shard_map/ppermute | solution.py:16
  175.7 57.1 %collective-permute-start.21 = (bf16[256,1024]{0,1:T(8,128)(2,1)S(1)}, bf16[256,1024]{0,1:T(8,128)(2,1)S(1)}, u32[]{:S(2)}, u32[]{:S(2)}) collective-permute-start(bf16[256,1024]{0,1:T(8,128)(2,1)S(1)} %bitcast.51), channel_id=1, source_target_pairs={{6,0},{7,1},{8,2},{9,3},{10,4},{11,5},{12,6},{13,7},{14,8},{15,9},... | collective-permute-start | bytes 1572872 | tf_op jit(solution)/shard_map/ppermute | solution.py:16
  180.9 81.3 %collective-permute-start.22 = (bf16[256,1024]{0,1:T(8,128)(2,1)S(1)}, bf16[256,1024]{0,1:T(8,128)(2,1)S(1)}, u32[]{:S(2)}, u32[]{:S(2)}) collective-permute-start(bf16[256,1024]{0,1:T(8,128)(2,1)S(1)} %bitcast.52), channel_id=1, source_target_pairs={{7,0},{8,1},{9,2},{10,3},{11,4},{12,5},{13,6},{14,7},{15,8},{16,9}... | collective-permute-start | bytes 1572872 | tf_op jit(solution)/shard_map/ppermute | solution.py:16
  194.8 70.5 %collective-permute-start.23 = (bf16[256,1024]{0,1:T(8,128)(2,1)S(1)}, bf16[256,1024]{0,1:T(8,128)(2,1)S(1)}, u32[]{:S(2)}, u32[]{:S(2)}) collective-permute-start(bf16[256,1024]{0,1:T(8,128)(2,1)S(1)} %bitcast.53), channel_id=1, source_target_pairs={{8,0},{9,1},{10,2},{11,3},{12,4},{13,5},{14,6},{15,7},{16,8},{17,9... | collective-permute-start | bytes 1572872 | tf_op jit(solution)/shard_map/ppermute | solution.py:16
  206.1 87.5 %collective-permute-start.24 = (bf16[256,1024]{0,1:T(8,128)(2,1)S(1)}, bf16[256,1024]{0,1:T(8,128)(2,1)S(1)}, u32[]{:S(2)}, u32[]{:S(2)}) collective-permute-start(bf16[256,1024]{0,1:T(8,128)(2,1)S(1)} %bitcast.54), channel_id=1, source_target_pairs={{9,0},{10,1},{11,2},{12,3},{13,4},{14,5},{15,6},{16,7},{17,8},{18,... | collective-permute-start | bytes 1572872 | tf_op jit(solution)/shard_map/ppermute | solution.py:16
  221.5 77.4 %collective-permute-start.25 = (bf16[256,1024]{0,1:T(8,128)(2,1)S(1)}, bf16[256,1024]{0,1:T(8,128)(2,1)S(1)}, u32[]{:S(2)}, u32[]{:S(2)}) collective-permute-start(bf16[256,1024]{0,1:T(8,128)(2,1)S(1)} %bitcast.55), channel_id=1, source_target_pairs={{10,0},{11,1},{12,2},{13,3},{14,4},{15,5},{16,6},{17,7},{18,8},{19... | collective-permute-start | bytes 1572872 | tf_op jit(solution)/shard_map/ppermute | solution.py:16
  232.8 76.5 %collective-permute-start.26 = (bf16[256,1024]{0,1:T(8,128)(2,1)S(1)}, bf16[256,1024]{0,1:T(8,128)(2,1)S(1)}, u32[]{:S(2)}, u32[]{:S(2)}) collective-permute-start(bf16[256,1024]{0,1:T(8,128)(2,1)S(1)} %bitcast.56), channel_id=1, source_target_pairs={{11,0},{12,1},{13,2},{14,3},{15,4},{16,5},{17,6},{18,7},{19,8},{20... | collective-permute-start | bytes 1572872 | tf_op jit(solution)/shard_map/ppermute | solution.py:16
  262.3 63.4 %collective-permute-start.27 = (bf16[256,1024]{0,1:T(8,128)(2,1)S(1)}, bf16[256,1024]{0,1:T(8,128)(2,1)S(1)}, u32[]{:S(2)}, u32[]{:S(2)}) collective-permute-start(bf16[256,1024]{0,1:T(8,128)(2,1)S(1)} %bitcast.57), channel_id=1, source_target_pairs={{12,0},{13,1},{14,2},{15,3},{16,4},{17,5},{18,6},{19,7},{20,8},{21... | collective-permute-start | bytes 1572872 | tf_op jit(solution)/shard_map/ppermute | solution.py:16
  265.3 69.4 %collective-permute-start.28 = (bf16[256,1024]{0,1:T(8,128)(2,1)S(1)}, bf16[256,1024]{0,1:T(8,128)(2,1)S(1)}, u32[]{:S(2)}, u32[]{:S(2)}) collective-permute-start(bf16[256,1024]{0,1:T(8,128)(2,1)S(1)} %bitcast.58), channel_id=1, source_target_pairs={{13,0},{14,1},{15,2},{16,3},{17,4},{18,5},{19,6},{20,7},{21,8},{22... | collective-permute-start | bytes 1572872 | tf_op jit(solution)/shard_map/ppermute | solution.py:16
  293.5 45.1 %collective-permute-start.29 = (bf16[256,1024]{0,1:T(8,128)(2,1)S(1)}, bf16[256,1024]{0,1:T(8,128)(2,1)S(1)}, u32[]{:S(2)}, u32[]{:S(2)}) collective-permute-start(bf16[256,1024]{0,1:T(8,128)(2,1)S(1)} %bitcast.59), channel_id=1, source_target_pairs={{14,0},{15,1},{16,2},{17,3},{18,4},{19,5},{20,6},{21,7},{22,8},{23... | collective-permute-start | bytes 1572872 | tf_op jit(solution)/shard_map/ppermute | solution.py:16
  299.0 75.2 %collective-permute-start.30 = (bf16[256,1024]{0,1:T(8,128)(2,1)S(1)}, bf16[256,1024]{0,1:T(8,128)(2,1)S(1)}, u32[]{:S(2)}, u32[]{:S(2)}) collective-permute-start(bf16[256,1024]{0,1:T(8,128)(2,1)S(1)} %bitcast.60), channel_id=1, source_target_pairs={{15,0},{16,1},{17,2},{18,3},{19,4},{20,5},{21,6},{22,7},{23,8},{24... | collective-permute-start | bytes 1572872 | tf_op jit(solution)/shard_map/ppermute | solution.py:16
  309.3 65.4 %collective-permute-start.31 = (bf16[256,1024]{0,1:T(8,128)(2,1)S(1)}, bf16[256,1024]{0,1:T(8,128)(2,1)S(1)}, u32[]{:S(2)}, u32[]{:S(2)}) collective-permute-start(bf16[256,1024]{0,1:T(8,128)(2,1)S(1)} %bitcast.61), channel_id=1, source_target_pairs={{16,0},{17,1},{18,2},{19,3},{20,4},{21,5},{22,6},{23,7},{24,8},{25... | collective-permute-start | bytes 1572872 | tf_op jit(solution)/shard_map/ppermute | solution.py:16
  374.6 15.5 %copy-start.1 = (bf16[8448,1024]{0,1:T(8,128)(2,1)}, bf16[8448,1024]{0,1:T(8,128)(2,1)S(1)}, u32[]{:S(2)}) copy-start(bf16[8448,1024]{0,1:T(8,128)(2,1)S(1)} %constant_dynamic-update-slice_fusion) | copy-start | bytes 51904516
  390.1 3.4 copy-start
  395.5 0.7 copy-start.3
  396.2 325.8 %all-reduce.7.cloned.1.call-start = ((), (), s32[]{:S(2)}) async-start(), calls=%async_computation.4 | async-start | bytes 327680 | tf_op jit(solution)/shard_map/psum | solution.py:81
  579.4 0.7 copy-start.4
  580.1 295.7 %all-reduce.9.cloned.1.call-start = ((), (), s32[]{:S(2)}) async-start(), calls=%async_computation.5 | async-start | bytes 327680 | tf_op jit(solution)/shard_map/psum | solution.py:81
  733.4 0.7 copy-start.2
  896.1 13.3 %all-to-all-start.2 = ((bf16[256,8,128]{2,0,1:T(8,128)(2,1)}), bf16[256,8,128]{2,0,1:T(8,128)(2,1)S(1)}, u32[]{:S(2)}, u32[]{:S(2)}) async-start(bf16[256,8,128]{2,0,1:T(8,128)(2,1)} %bitcast.27), calls=%async_computation.2 | async-start | bytes 1048576 | tf_op jit(solution)/shard_map/all_to_all | solution.py:97
Sparse Core Ops, SparseCore 0:
  396.3 171.6 all-reduce.4
  580.2 141.6 all-reduce.6
  734.2 141.6 all-reduce.8
where the time goes:
time: 918 us; the launch traced here: 917 us
  waiting for transfers between devices  702 us (76%)
  starting transfers between devices  127 us (14%)
  other arithmetic  35.1 us (4%)
  matrix products  24.3 us (3%)
  between operations  14.5 us (2%)
  local copies, waits for them, and re-layouts  14.1 us (2%)
    psum x3, waiting for transfers between devices, column_scaling(): columns = lax.psum(full, ('seq', 'emb'))  455 us
    ppermute x32, waiting for transfers between devices, shifted_2(): return lax.ppermute(block, axis, route)  228 us
    ppermute x32, starting transfers between devices, shifted_2(): return lax.ppermute(block, axis, route)  112 us
  transfers between devices with their start and end apart: 38, of which 28 were waited for; matrix products, arithmetic and copies ran while one was open for 1% of the time, Pallas kernels for 0%

commit v1 on v0

--- a/solution.py
+++ b/solution.py
@@ -1,3 +1,4 @@
+import functools
 import jax
 import jax.numpy as jnp
 from jax import lax
@@ -8,6 +9,14 @@
 ITERS = 3
 INV_EPS = 50.0
 PENALTY = 0.04
+
+
+def _deliver_patches(s0, peer_axis):
+    next_value = lax.all_gather(s0, peer_axis).sum(axis=0)
+    return next_value
+
+
+match_halves = functools.partial(_deliver_patches, peer_axis=("seq", "emb"))
 
 
 def shifted_2(block, axis, distance):
@@ -78,7 +87,7 @@
         full = lax.dynamic_update_slice_in_dim(
             jnp.zeros((padded_len,), jnp.float32), part, first_row, 0
         )
-        columns = lax.psum(full, ("seq", "emb"))
+        columns = match_halves(full)
         mine = lax.dynamic_slice_in_dim(columns, first_row, width, 0)
         return jnp.where(valid, 1.0 / jnp.where(valid, mine, 1.0), 0.0)
 

time: 918 us -> 792 us (0.86)
  waiting for transfers between devices: 702 us -> 534 us
  other arithmetic: 35.1 us -> 78.7 us
    psum x3 -> x0, waiting for transfers between devices: 455 us -> none  [column_scaling(): columns = lax.psum(full, ('seq', 'emb'))]
    all_gather x0 -> x3, waiting for transfers between devices: none -> 288 us  [_deliver_patches(): next_value = lax.all_gather(s0, peer_axis).sum(axis=0)]
    reduce_sum x0 -> x3, other arithmetic: none -> 45.9 us  [_deliver_patches(): next_value = lax.all_gather(s0, peer_axis).sum(axis=0)]
where the time goes in v1:
time: 792 us; the launch traced here: 791 us
  waiting for transfers between devices  534 us (67%)
  starting transfers between devices  127 us (16%)
  other arithmetic  78.7 us (10%)
  matrix products  24.2 us (3%)
  between operations  14.5 us (2%)
  local copies, waits for them, and re-layouts  12.7 us (2%)
    all_gather x3, waiting for transfers between devices, _deliver_patches(): next_value = lax.all_gather(s0, peer_axis).sum(axis=0)  288 us
    ppermute x32, waiting for transfers between devices, shifted_2(): return lax.ppermute(block, axis, route)  228 us
    ppermute x32, starting transfers between devices, shifted_2(): return lax.ppermute(block, axis, route)  112 us
    reduce_sum x3, other arithmetic, _deliver_patches(): next_value = lax.all_gather(s0, peer_axis).sum(axis=0)  45.9 us
  transfers between devices with their start and end apart: 38, of which 28 were waited for; matrix products, arithmetic and copies ran while one was open for 1% of the time, Pallas kernels for 0%

profile of v1, /device:TPU:1, one launch (start us, length us, event | category | flops | bytes accessed | tf_op | source)
XLA Modules:
  0.0 790.9 jit_solution(408196945838685765)
XLA Ops:
  7.2 6.8 all-to-all-start
  14.0 9.3 %all-to-all-done = bf16[8,256,128]{2,1,0:T(8,128)(2,1)S(1)} async-done(((bf16[8,256,128]{2,1,0:T(8,128)(2,1)}), bf16[8,256,128]{2,1,0:T(8,128)(2,1)S(1)}, u32[]{:S(2)}, u32[]{:S(2)}) %all-to-all-start) | async-done | bytes 524320 | tf_op jit(solution)/shard_map/all_to_all | solution.py:38
  23.3 4.4 all-to-all-start.1
  28.7 5.5 collective-permute-start
  38.6 6.4 collective-permute-start.2
  48.3 4.7 collective-permute-start.4
  53.4 6.1 collective-permute-start.5
  62.5 4.5 collective-permute-done.2
  67.1 5.0 collective-permute-start.7
  73.2 5.1 collective-permute-done.3
  79.6 9.9 %collective-permute-done.4 = bf16[256,1024]{0,1:T(8,128)(2,1)S(1)} collective-permute-done((bf16[256,1024]{0,1:T(8,128)(2,1)S(1)}, bf16[256,1024]{0,1:T(8,128)(2,1)S(1)}, u32[]{:S(2)}, u32[]{:S(2)}) %collective-permute-start.4) | collective-permute-done | bytes 524320 | tf_op jit(solution)/shard_map/ppermute | solution.py:25
  89.5 11.1 %collective-permute-start.9 = (bf16[256,1024]{0,1:T(8,128)(2,1)S(1)}, bf16[256,1024]{0,1:T(8,128)(2,1)S(1)}, u32[]{:S(2)}, u32[]{:S(2)}) collective-permute-start(bf16[256,1024]{0,1:T(8,128)(2,1)S(1)} %bitcast.38), channel_id=1, source_target_pairs={{0,7},{1,8},{2,9},{3,10},{4,11},{5,12},{6,13},{7,14},{8,15},{9,16}... | collective-permute-start | bytes 1572872 | tf_op jit(solution)/shard_map/ppermute | solution.py:25
  100.8 4.3 collective-permute-start.10
  105.1 6.9 collective-permute-done.6
  112.0 6.5 collective-permute-start.11
  118.5 4.7 collective-permute-done.7
  123.2 4.6 collective-permute-start.12
  127.9 6.6 collective-permute-done.8
  134.5 6.6 collective-permute-start.13
  141.1 7.7 collective-permute-start.14
  148.8 13.2 %collective-permute-start.15 = (bf16[256,1024]{0,1:T(8,128)(2,1)S(1)}, bf16[256,1024]{0,1:T(8,128)(2,1)S(1)}, u32[]{:S(2)}, u32[]{:S(2)}) collective-permute-start(bf16[256,1024]{0,1:T(8,128)(2,1)S(1)} %bitcast.44), channel_id=1, source_target_pairs={{0,1},{1,2},{2,3},{3,4},{4,5},{5,6},{6,7},{7,8},{8,9},{9,10},{10,1... | collective-permute-start | bytes 1572872 | tf_op jit(solution)/shard_map/ppermute | solution.py:25
  169.5 6.2 collective-permute-done.16
  182.3 12.5 %collective-permute-done.18 = bf16[256,1024]{0,1:T(8,128)(2,1)S(1)} collective-permute-done((bf16[256,1024]{0,1:T(8,128)(2,1)S(1)}, bf16[256,1024]{0,1:T(8,128)(2,1)S(1)}, u32[]{:S(2)}, u32[]{:S(2)}) %collective-permute-start.18) | collective-permute-done | bytes 524320 | tf_op jit(solution)/shard_map/ppermute | solution.py:25
  196.2 9.9 %collective-permute-done.19 = bf16[256,1024]{0,1:T(8,128)(2,1)S(1)} collective-permute-done((bf16[256,1024]{0,1:T(8,128)(2,1)S(1)}, bf16[256,1024]{0,1:T(8,128)(2,1)S(1)}, u32[]{:S(2)}, u32[]{:S(2)}) %collective-permute-start.19) | collective-permute-done | bytes 524320 | tf_op jit(solution)/shard_map/ppermute | solution.py:25
  207.4 14.2 %collective-permute-done.20 = bf16[256,1024]{0,1:T(8,128)(2,1)S(1)} collective-permute-done((bf16[256,1024]{0,1:T(8,128)(2,1)S(1)}, bf16[256,1024]{0,1:T(8,128)(2,1)S(1)}, u32[]{:S(2)}, u32[]{:S(2)}) %collective-permute-start.20) | collective-permute-done | bytes 524320 | tf_op jit(solution)/shard_map/ppermute | solution.py:25
  222.9 9.9 %collective-permute-done.21 = bf16[256,1024]{0,1:T(8,128)(2,1)S(1)} collective-permute-done((bf16[256,1024]{0,1:T(8,128)(2,1)S(1)}, bf16[256,1024]{0,1:T(8,128)(2,1)S(1)}, u32[]{:S(2)}, u32[]{:S(2)}) %collective-permute-start.21) | collective-permute-done | bytes 524320 | tf_op jit(solution)/shard_map/ppermute | solution.py:25
  234.1 28.2 %collective-permute-done.22 = bf16[256,1024]{0,1:T(8,128)(2,1)S(1)} collective-permute-done((bf16[256,1024]{0,1:T(8,128)(2,1)S(1)}, bf16[256,1024]{0,1:T(8,128)(2,1)S(1)}, u32[]{:S(2)}, u32[]{:S(2)}) %collective-permute-start.22) | collective-permute-done | bytes 524320 | tf_op jit(solution)/shard_map/ppermute | solution.py:25
  266.6 26.9 %collective-permute-done.24 = bf16[256,1024]{0,1:T(8,128)(2,1)S(1)} collective-permute-done((bf16[256,1024]{0,1:T(8,128)(2,1)S(1)}, bf16[256,1024]{0,1:T(8,128)(2,1)S(1)}, u32[]{:S(2)}, u32[]{:S(2)}) %collective-permute-start.24) | collective-permute-done | bytes 524320 | tf_op jit(solution)/shard_map/ppermute | solution.py:25
  294.9 4.1 collective-permute-done.25
  300.3 8.9 %collective-permute-done.26 = bf16[256,1024]{0,1:T(8,128)(2,1)S(1)} collective-permute-done((bf16[256,1024]{0,1:T(8,128)(2,1)S(1)}, bf16[256,1024]{0,1:T(8,128)(2,1)S(1)}, u32[]{:S(2)}, u32[]{:S(2)}) %collective-permute-start.26) | collective-permute-done | bytes 524320 | tf_op jit(solution)/shard_map/ppermute | solution.py:25
  310.6 15.1 %collective-permute-done.27 = bf16[256,1024]{0,1:T(8,128)(2,1)S(1)} collective-permute-done((bf16[256,1024]{0,1:T(8,128)(2,1)S(1)}, bf16[256,1024]{0,1:T(8,128)(2,1)S(1)}, u32[]{:S(2)}, u32[]{:S(2)}) %collective-permute-start.27) | collective-permute-done | bytes 524320 | tf_op jit(solution)/shard_map/ppermute | solution.py:25
  325.7 8.9 %collective-permute-done.28 = bf16[256,1024]{0,1:T(8,128)(2,1)S(1)} collective-permute-done((bf16[256,1024]{0,1:T(8,128)(2,1)S(1)}, bf16[256,1024]{0,1:T(8,128)(2,1)S(1)}, u32[]{:S(2)}, u32[]{:S(2)}) %collective-permute-start.28) | collective-permute-done | bytes 524320 | tf_op jit(solution)/shard_map/ppermute | solution.py:25
  334.7 4.0 collective-permute-done.29
  338.7 35.5 %collective-permute-done.30 = bf16[256,1024]{0,1:T(8,128)(2,1)S(1)} collective-permute-done((bf16[256,1024]{0,1:T(8,128)(2,1)S(1)}, bf16[256,1024]{0,1:T(8,128)(2,1)S(1)}, u32[]{:S(2)}, u32[]{:S(2)}) %collective-permute-start.30) | collective-permute-done | bytes 524320 | tf_op jit(solution)/shard_map/ppermute | solution.py:25
  378.6 11.5 %multiply_reduce_fusion.6 = (f32[256]{0:T(256)S(1)}, f32[256,8448]{0,1:T(8,128)S(1)}) fusion(f32[8448]{0:T(1024)S(1)} %get-tuple-element.5, s32[8448]{0:T(1024)S(1)} %get-tuple-element.6, s32[256]{0:T(256)S(1)} %dynamic_slice.15, f32[8448]{0:T(1024)S(1)} %add_rsqrt_fusion, f32[256]{0:T(256)S(1)} %add_rsqrt_fusion.1, ...), kind=kOutput, calls=%fused_computation.14 | convolution fusion | flops 4459462656 | bytes 26625280 | tf_op jit(solution)/shard_map/dot_general | solution.py:73
  395.7 115.1 %all-gather.7.cloned.1.call-done = f32[128,1,40960]{2,1,0:T(1,128)} async-done(((f32[1,1,40960]{2,1,0:T(1,128)}), f32[128,1,40960]{2,1,0:T(1,128)}) %all-gather.7.cloned.1.call-update) | async-done | bytes 20971536 | tf_op jit(solution)/shard_map/all_gather | solution.py:15
  510.8 15.3 %reduce_sum.112 = f32[40960]{0:T(1024)S(1)} reduce(f32[128,1,40960]{2,1,0:T(1,128)} %all-gather.7.cloned.1.call-done, f32[]{:T(128)} %constant.10.clone.1), dimensions={0,1}, to_apply=%region_4.5 | reduce | flops 5201920 | bytes 21135364 | tf_op jit(solution)/shard_map/reduce_sum | solution.py:15
  526.2 5.7 multiply_reduce_fusion.4
  532.0 4.2 multiply_reduce_fusion.3
  537.1 86.2 %all-gather.9.cloned.1.call-done = f32[128,1,40960]{2,1,0:T(1,128)} async-done(((f32[1,1,40960]{2,1,0:T(1,128)}), f32[128,1,40960]{2,1,0:T(1,128)}) %all-gather.9.cloned.1.call-update) | async-done | bytes 20971536 | tf_op jit(solution)/shard_map/all_gather | solution.py:15
  623.3 15.3 %reduce_sum.115 = f32[40960]{0:T(1024)S(1)} reduce(f32[128,1,40960]{2,1,0:T(1,128)} %all-gather.9.cloned.1.call-done, f32[]{:T(128)} %constant.10.clone.1), dimensions={0,1}, to_apply=%region_7.8 | reduce | flops 5201920 | bytes 21135364 | tf_op jit(solution)/shard_map/reduce_sum | solution.py:15
  638.7 5.7 multiply_reduce_fusion.2
  644.4 4.2 multiply_reduce_fusion.1
  649.4 86.3 %all-gather.11.cloned.1.call-done = f32[128,1,40960]{2,1,0:T(1,128)} async-done(((f32[1,1,40960]{2,1,0:T(1,128)}), f32[128,1,40960]{2,1,0:T(1,128)}) %all-gather.11.cloned.1.call-update) | async-done | bytes 20971536 | tf_op jit(solution)/shard_map/all_gather | solution.py:15
  735.7 15.3 %reduce_sum.118 = f32[40960]{0:T(1024)S(1)} reduce(f32[128,1,40960]{2,1,0:T(1,128)} %all-gather.11.cloned.1.call-done, f32[]{:T(128)} %constant.10.clone.1), dimensions={0,1}, to_apply=%region_10.11 | reduce | flops 5201920 | bytes 21135364 | tf_op jit(solution)/shard_map/reduce_sum | solution.py:15
  751.1 5.7 multiply_reduce_fusion.7
  756.8 12.8 %fusion.11 = bf16[32,8,8,128]{3,2,1,0:T(8,128)(2,1)S(1)} fusion(bf16[8448,1024]{0,1:T(8,128)(2,1)} %copy-done.1, f32[256,8448]{0,1:T(8,128)} %copy-done, f32[256]{0:T(256)S(1)} %multiply_reduce_fusion.7, f32[8448]{0:T(1024)S(1)} %divide_select_fusion), kind=kOutput, calls=%fused_computation.22 | convolution fusion | flops 4435935232 | bytes 26511360 | tf_op jit(solution)/shard_map/dot_general | solution.py:105
  774.7 8.8 %all-to-all-done.2 = bf16[256,8,128]{2,0,1:T(8,128)(2,1)S(1)} async-done(((bf16[256,8,128]{2,0,1:T(8,128)(2,1)}), bf16[256,8,128]{2,0,1:T(8,128)(2,1)S(1)}, u32[]{:S(2)}, u32[]{:S(2)}) %all-to-all-start.2) | async-done | bytes 524320 | tf_op jit(solution)/shard_map/all_to_all | solution.py:106
  (112 shorter events, 60.1 us)
Async XLA Ops:
  7.2 16.2 %all-to-all-start = ((bf16[8,256,128]{2,1,0:T(8,128)(2,1)}), bf16[8,256,128]{2,1,0:T(8,128)(2,1)S(1)}, u32[]{:S(2)}, u32[]{:S(2)}) async-start(bf16[8,256,128]{2,1,0:T(8,128)(2,1)} %bitcast.64), calls=%async_computation | async-start | bytes 1048576 | tf_op jit(solution)/shard_map/all_to_all | solution.py:38
  23.3 29.6 %all-to-all-start.1 = ((bf16[8,256,128]{2,1,0:T(8,128)(2,1)}), bf16[8,256,128]{2,1,0:T(8,128)(2,1)S(1)}, u32[]{:S(2)}, u32[]{:S(2)}) async-start(bf16[8,256,128]{2,1,0:T(8,128)(2,1)} %bitcast.65), calls=%async_computation.1 | async-start | bytes 1048576 | tf_op jit(solution)/shard_map/all_to_all | solution.py:37
  27.7 483.1 %all-gather.7.cloned.1.call-start = ((), (), s32[]{:S(2)}) async-start(), calls=%async_computation.3 | async-start | bytes 21135360 | tf_op jit(solution)/shard_map/all_gather | solution.py:15
  28.7 24.6 %collective-permute-start = (bf16[256,1024]{0,1:T(8,128)(2,1)S(1)}, bf16[256,1024]{0,1:T(8,128)(2,1)}, u32[]{:S(2)}, u32[]{:S(2)}) collective-permute-start(bf16[256,1024]{0,1:T(8,128)(2,1)S(1)} %bitcast.29), channel_id=1, source_target_pairs={{0,16},{1,17},{2,18},{3,19},{4,20},{5,21},{6,22},{7,23},{8,24},{9,... | collective-permute-start | bytes 1572872 | tf_op jit(solution)/shard_map/ppermute | solution.py:25
  34.3 26.3 %collective-permute-start.1 = (bf16[256,1024]{0,1:T(8,128)(2,1)S(1)}, bf16[256,1024]{0,1:T(8,128)(2,1)S(1)}, u32[]{:S(2)}, u32[]{:S(2)}) collective-permute-start(bf16[256,1024]{0,1:T(8,128)(2,1)S(1)} %bitcast.30), channel_id=1, source_target_pairs={{0,15},{1,16},{2,17},{3,18},{4,19},{5,20},{6,21},{7,22},{8,23},{9,... | collective-permute-start | bytes 1572872 | tf_op jit(solution)/shard_map/ppermute | solution.py:25
  38.6 28.5 %collective-permute-start.2 = (bf16[256,1024]{0,1:T(8,128)(2,1)S(1)}, bf16[256,1024]{0,1:T(8,128)(2,1)}, u32[]{:S(2)}, u32[]{:S(2)}) collective-permute-start(bf16[256,1024]{0,1:T(8,128)(2,1)S(1)} %bitcast.31), channel_id=1, source_target_pairs={{0,14},{1,15},{2,16},{3,17},{4,18},{5,19},{6,20},{7,21},{8,22},{9,... | collective-permute-start | bytes 1572872 | tf_op jit(solution)/shard_map/ppermute | solution.py:25
  45.0 33.3 %collective-permute-start.3 = (bf16[256,1024]{0,1:T(8,128)(2,1)S(1)}, bf16[256,1024]{0,1:T(8,128)(2,1)S(1)}, u32[]{:S(2)}, u32[]{:S(2)}) collective-permute-start(bf16[256,1024]{0,1:T(8,128)(2,1)S(1)} %bitcast.32), channel_id=1, source_target_pairs={{0,13},{1,14},{2,15},{3,16},{4,17},{5,18},{6,19},{7,20},{8,21},{9,... | collective-permute-start | bytes 1572872 | tf_op jit(solution)/shard_map/ppermute | solution.py:25
  48.3 41.3 %collective-permute-start.4 = (bf16[256,1024]{0,1:T(8,128)(2,1)S(1)}, bf16[256,1024]{0,1:T(8,128)(2,1)S(1)}, u32[]{:S(2)}, u32[]{:S(2)}) collective-permute-start(bf16[256,1024]{0,1:T(8,128)(2,1)S(1)} %bitcast.33), channel_id=1, source_target_pairs={{0,12},{1,13},{2,14},{3,15},{4,16},{5,17},{6,18},{7,19},{8,20},{9,... | collective-permute-start | bytes 1572872 | tf_op jit(solution)/shard_map/ppermute | solution.py:25
  53.4 47.4 %collective-permute-start.5 = (bf16[256,1024]{0,1:T(8,128)(2,1)S(1)}, bf16[256,1024]{0,1:T(8,128)(2,1)S(1)}, u32[]{:S(2)}, u32[]{:S(2)}) collective-permute-start(bf16[256,1024]{0,1:T(8,128)(2,1)S(1)} %bitcast.34), channel_id=1, source_target_pairs={{0,11},{1,12},{2,13},{3,14},{4,15},{5,16},{6,17},{7,18},{8,19},{9,... | collective-permute-start | bytes 1572872 | tf_op jit(solution)/shard_map/ppermute | solution.py:25
  60.5 51.5 %collective-permute-start.6 = (bf16[256,1024]{0,1:T(8,128)(2,1)S(1)}, bf16[256,1024]{0,1:T(8,128)(2,1)S(1)}, u32[]{:S(2)}, u32[]{:S(2)}) collective-permute-start(bf16[256,1024]{0,1:T(8,128)(2,1)S(1)} %bitcast.35), channel_id=1, source_target_pairs={{0,10},{1,11},{2,12},{3,13},{4,14},{5,15},{6,16},{7,17},{8,18},{9,... | collective-permute-start | bytes 1572872 | tf_op jit(solution)/shard_map/ppermute | solution.py:25
  67.1 56.2 %collective-permute-start.7 = (bf16[256,1024]{0,1:T(8,128)(2,1)S(1)}, bf16[256,1024]{0,1:T(8,128)(2,1)S(1)}, u32[]{:S(2)}, u32[]{:S(2)}) collective-permute-start(bf16[256,1024]{0,1:T(8,128)(2,1)S(1)} %bitcast.36), channel_id=1, source_target_pairs={{0,9},{1,10},{2,11},{3,12},{4,13},{5,14},{6,15},{7,16},{8,17},{9,1... | collective-permute-start | bytes 1572872 | tf_op jit(solution)/shard_map/ppermute | solution.py:25
  78.3 56.2 %collective-permute-start.8 = (bf16[256,1024]{0,1:T(8,128)(2,1)S(1)}, bf16[256,1024]{0,1:T(8,128)(2,1)S(1)}, u32[]{:S(2)}, u32[]{:S(2)}) collective-permute-start(bf16[256,1024]{0,1:T(8,128)(2,1)S(1)} %bitcast.37), channel_id=1, source_target_pairs={{0,8},{1,9},{2,10},{3,11},{4,12},{5,13},{6,14},{7,15},{8,16},{9,17... | collective-permute-start | bytes 1572872 | tf_op jit(solution)/shard_map/ppermute | solution.py:25
  89.5 51.6 %collective-permute-start.9 = (bf16[256,1024]{0,1:T(8,128)(2,1)S(1)}, bf16[256,1024]{0,1:T(8,128)(2,1)S(1)}, u32[]{:S(2)}, u32[]{:S(2)}) collective-permute-start(bf16[256,1024]{0,1:T(8,128)(2,1)S(1)} %bitcast.38), channel_id=1, source_target_pairs={{0,7},{1,8},{2,9},{3,10},{4,11},{5,12},{6,13},{7,14},{8,15},{9,16}... | collective-permute-start | bytes 1572872 | tf_op jit(solution)/shard_map/ppermute | solution.py:25
  100.8 48.1 %collective-permute-start.10 = (bf16[256,1024]{0,1:T(8,128)(2,1)S(1)}, bf16[256,1024]{0,1:T(8,128)(2,1)S(1)}, u32[]{:S(2)}, u32[]{:S(2)}) collective-permute-start(bf16[256,1024]{0,1:T(8,128)(2,1)S(1)} %bitcast.39), channel_id=1, source_target_pairs={{0,6},{1,7},{2,8},{3,9},{4,10},{5,11},{6,12},{7,13},{8,14},{9,15},... | collective-permute-start | bytes 1572872 | tf_op jit(solution)/shard_map/ppermute | solution.py:25
  112.0 50.1 %collective-permute-start.11 = (bf16[256,1024]{0,1:T(8,128)(2,1)S(1)}, bf16[256,1024]{0,1:T(8,128)(2,1)S(1)}, u32[]{:S(2)}, u32[]{:S(2)}) collective-permute-start(bf16[256,1024]{0,1:T(8,128)(2,1)S(1)} %bitcast.40), channel_id=1, source_target_pairs={{0,5},{1,6},{2,7},{3,8},{4,9},{5,10},{6,11},{7,12},{8,13},{9,14},{... | collective-permute-start | bytes 1572872 | tf_op jit(solution)/shard_map/ppermute | solution.py:25
  123.2 40.8 %collective-permute-start.12 = (bf16[256,1024]{0,1:T(8,128)(2,1)S(1)}, bf16[256,1024]{0,1:T(8,128)(2,1)S(1)}, u32[]{:S(2)}, u32[]{:S(2)}) collective-permute-start(bf16[256,1024]{0,1:T(8,128)(2,1)S(1)} %bitcast.41), channel_id=1, source_target_pairs={{0,4},{1,5},{2,6},{3,7},{4,8},{5,9},{6,10},{7,11},{8,12},{9,13},{1... | collective-permute-start | bytes 1572872 | tf_op jit(solution)/shard_map/ppermute | solution.py:25
  134.5 30.9 %collective-permute-start.13 = (bf16[256,1024]{0,1:T(8,128)(2,1)S(1)}, bf16[256,1024]{0,1:T(8,128)(2,1)S(1)}, u32[]{:S(2)}, u32[]{:S(2)}) collective-permute-start(bf16[256,1024]{0,1:T(8,128)(2,1)S(1)} %bitcast.42), channel_id=1, source_target_pairs={{0,3},{1,4},{2,5},{3,6},{4,7},{5,8},{6,9},{7,10},{8,11},{9,12},{10... | collective-permute-start | bytes 1572872 | tf_op jit(solution)/shard_map/ppermute | solution.py:25
  141.1 25.7 %collective-permute-start.14 = (bf16[256,1024]{0,1:T(8,128)(2,1)S(1)}, bf16[256,1024]{0,1:T(8,128)(2,1)S(1)}, u32[]{:S(2)}, u32[]{:S(2)}) collective-permute-start(bf16[256,1024]{0,1:T(8,128)(2,1)S(1)} %bitcast.43), channel_id=1, source_target_pairs={{0,2},{1,3},{2,4},{3,5},{4,6},{5,7},{6,8},{7,9},{8,10},{9,11},{10,... | collective-permute-start | bytes 1572872 | tf_op jit(solution)/shard_map/ppermute | solution.py:25
  148.8 19.3 %collective-permute-start.15 = (bf16[256,1024]{0,1:T(8,128)(2,1)S(1)}, bf16[256,1024]{0,1:T(8,128)(2,1)S(1)}, u32[]{:S(2)}, u32[]{:S(2)}) collective-permute-start(bf16[256,1024]{0,1:T(8,128)(2,1)S(1)} %bitcast.44), channel_id=1, source_target_pairs={{0,1},{1,2},{2,3},{3,4},{4,5},{5,6},{6,7},{7,8},{8,9},{9,10},{10,1... | collective-permute-start | bytes 1572872 | tf_op jit(solution)/shard_map/ppermute | solution.py:25
  162.1 13.6 %collective-permute-start.16 = (bf16[256,1024]{0,1:T(8,128)(2,1)S(1)}, bf16[256,1024]{0,1:T(8,128)(2,1)S(1)}, u32[]{:S(2)}, u32[]{:S(2)}) collective-permute-start(bf16[256,1024]{0,1:T(8,128)(2,1)S(1)} %bitcast.45), channel_id=1, source_target_pairs={{1,0},{2,1},{3,2},{4,3},{5,4},{6,5},{7,6},{8,7},{9,8},{10,9},{11,1... | collective-permute-start | bytes 1572872 | tf_op jit(solution)/shard_map/ppermute | solution.py:25
  164.0 16.9 %collective-permute-start.17 = (bf16[256,1024]{0,1:T(8,128)(2,1)S(1)}, bf16[256,1024]{0,1:T(8,128)(2,1)S(1)}, u32[]{:S(2)}, u32[]{:S(2)}) collective-permute-start(bf16[256,1024]{0,1:T(8,128)(2,1)S(1)} %bitcast.46), channel_id=1, source_target_pairs={{2,0},{3,1},{4,2},{5,3},{6,4},{7,5},{8,6},{9,7},{10,8},{11,9},{12,... | collective-permute-start | bytes 1572872 | tf_op jit(solution)/shard_map/ppermute | solution.py:25
  165.4 29.4 %collective-permute-start.18 = (bf16[256,1024]{0,1:T(8,128)(2,1)S(1)}, bf16[256,1024]{0,1:T(8,128)(2,1)S(1)}, u32[]{:S(2)}, u32[]{:S(2)}) collective-permute-start(bf16[256,1024]{0,1:T(8,128)(2,1)S(1)} %bitcast.47), channel_id=1, source_target_pairs={{3,0},{4,1},{5,2},{6,3},{7,4},{8,5},{9,6},{10,7},{11,8},{12,9},{13... | collective-permute-start | bytes 1572872 | tf_op jit(solution)/shard_map/ppermute | solution.py:25
  166.7 39.3 %collective-permute-start.19 = (bf16[256,1024]{0,1:T(8,128)(2,1)S(1)}, bf16[256,1024]{0,1:T(8,128)(2,1)S(1)}, u32[]{:S(2)}, u32[]{:S(2)}) collective-permute-start(bf16[256,1024]{0,1:T(8,128)(2,1)S(1)} %bitcast.48), channel_id=1, source_target_pairs={{4,0},{5,1},{6,2},{7,3},{8,4},{9,5},{10,6},{11,7},{12,8},{13,9},{1... | collective-permute-start | bytes 1572872 | tf_op jit(solution)/shard_map/ppermute | solution.py:25
  168.1 53.4 %collective-permute-start.20 = (bf16[256,1024]{0,1:T(8,128)(2,1)S(1)}, bf16[256,1024]{0,1:T(8,128)(2,1)S(1)}, u32[]{:S(2)}, u32[]{:S(2)}) collective-permute-start(bf16[256,1024]{0,1:T(8,128)(2,1)S(1)} %bitcast.49), channel_id=1, source_target_pairs={{5,0},{6,1},{7,2},{8,3},{9,4},{10,5},{11,6},{12,7},{13,8},{14,9},{... | collective-permute-start | bytes 1572872 | tf_op jit(solution)/shard_map/ppermute | solution.py:25
  175.7 57.1 %collective-permute-start.21 = (bf16[256,1024]{0,1:T(8,128)(2,1)S(1)}, bf16[256,1024]{0,1:T(8,128)(2,1)S(1)}, u32[]{:S(2)}, u32[]{:S(2)}) collective-permute-start(bf16[256,1024]{0,1:T(8,128)(2,1)S(1)} %bitcast.51), channel_id=1, source_target_pairs={{6,0},{7,1},{8,2},{9,3},{10,4},{11,5},{12,6},{13,7},{14,8},{15,9},... | collective-permute-start | bytes 1572872 | tf_op jit(solution)/shard_map/ppermute | solution.py:25
  180.9 81.3 %collective-permute-start.22 = (bf16[256,1024]{0,1:T(8,128)(2,1)S(1)}, bf16[256,1024]{0,1:T(8,128)(2,1)S(1)}, u32[]{:S(2)}, u32[]{:S(2)}) collective-permute-start(bf16[256,1024]{0,1:T(8,128)(2,1)S(1)} %bitcast.52), channel_id=1, source_target_pairs={{7,0},{8,1},{9,2},{10,3},{11,4},{12,5},{13,6},{14,7},{15,8},{16,9}... | collective-permute-start | bytes 1572872 | tf_op jit(solution)/shard_map/ppermute | solution.py:25
  194.8 70.5 %collective-permute-start.23 = (bf16[256,1024]{0,1:T(8,128)(2,1)S(1)}, bf16[256,1024]{0,1:T(8,128)(2,1)S(1)}, u32[]{:S(2)}, u32[]{:S(2)}) collective-permute-start(bf16[256,1024]{0,1:T(8,128)(2,1)S(1)} %bitcast.53), channel_id=1, source_target_pairs={{8,0},{9,1},{10,2},{11,3},{12,4},{13,5},{14,6},{15,7},{16,8},{17,9... | collective-permute-start | bytes 1572872 | tf_op jit(solution)/shard_map/ppermute | solution.py:25
  206.1 87.5 %collective-permute-start.24 = (bf16[256,1024]{0,1:T(8,128)(2,1)S(1)}, bf16[256,1024]{0,1:T(8,128)(2,1)S(1)}, u32[]{:S(2)}, u32[]{:S(2)}) collective-permute-start(bf16[256,1024]{0,1:T(8,128)(2,1)S(1)} %bitcast.54), channel_id=1, source_target_pairs={{9,0},{10,1},{11,2},{12,3},{13,4},{14,5},{15,6},{16,7},{17,8},{18,... | collective-permute-start | bytes 1572872 | tf_op jit(solution)/shard_map/ppermute | solution.py:25
  221.5 77.4 %collective-permute-start.25 = (bf16[256,1024]{0,1:T(8,128)(2,1)S(1)}, bf16[256,1024]{0,1:T(8,128)(2,1)S(1)}, u32[]{:S(2)}, u32[]{:S(2)}) collective-permute-start(bf16[256,1024]{0,1:T(8,128)(2,1)S(1)} %bitcast.55), channel_id=1, source_target_pairs={{10,0},{11,1},{12,2},{13,3},{14,4},{15,5},{16,6},{17,7},{18,8},{19... | collective-permute-start | bytes 1572872 | tf_op jit(solution)/shard_map/ppermute | solution.py:25
  232.8 76.5 %collective-permute-start.26 = (bf16[256,1024]{0,1:T(8,128)(2,1)S(1)}, bf16[256,1024]{0,1:T(8,128)(2,1)S(1)}, u32[]{:S(2)}, u32[]{:S(2)}) collective-permute-start(bf16[256,1024]{0,1:T(8,128)(2,1)S(1)} %bitcast.56), channel_id=1, source_target_pairs={{11,0},{12,1},{13,2},{14,3},{15,4},{16,5},{17,6},{18,7},{19,8},{20... | collective-permute-start | bytes 1572872 | tf_op jit(solution)/shard_map/ppermute | solution.py:25
  262.3 63.4 %collective-permute-start.27 = (bf16[256,1024]{0,1:T(8,128)(2,1)S(1)}, bf16[256,1024]{0,1:T(8,128)(2,1)S(1)}, u32[]{:S(2)}, u32[]{:S(2)}) collective-permute-start(bf16[256,1024]{0,1:T(8,128)(2,1)S(1)} %bitcast.57), channel_id=1, source_target_pairs={{12,0},{13,1},{14,2},{15,3},{16,4},{17,5},{18,6},{19,7},{20,8},{21... | collective-permute-start | bytes 1572872 | tf_op jit(solution)/shard_map/ppermute | solution.py:25
  265.3 69.4 %collective-permute-start.28 = (bf16[256,1024]{0,1:T(8,128)(2,1)S(1)}, bf16[256,1024]{0,1:T(8,128)(2,1)S(1)}, u32[]{:S(2)}, u32[]{:S(2)}) collective-permute-start(bf16[256,1024]{0,1:T(8,128)(2,1)S(1)} %bitcast.58), channel_id=1, source_target_pairs={{13,0},{14,1},{15,2},{16,3},{17,4},{18,5},{19,6},{20,7},{21,8},{22... | collective-permute-start | bytes 1572872 | tf_op jit(solution)/shard_map/ppermute | solution.py:25
  293.5 45.1 %collective-permute-start.29 = (bf16[256,1024]{0,1:T(8,128)(2,1)S(1)}, bf16[256,1024]{0,1:T(8,128)(2,1)S(1)}, u32[]{:S(2)}, u32[]{:S(2)}) collective-permute-start(bf16[256,1024]{0,1:T(8,128)(2,1)S(1)} %bitcast.59), channel_id=1, source_target_pairs={{14,0},{15,1},{16,2},{17,3},{18,4},{19,5},{20,6},{21,7},{22,8},{23... | collective-permute-start | bytes 1572872 | tf_op jit(solution)/shard_map/ppermute | solution.py:25
  299.0 75.2 %collective-permute-start.30 = (bf16[256,1024]{0,1:T(8,128)(2,1)S(1)}, bf16[256,1024]{0,1:T(8,128)(2,1)S(1)}, u32[]{:S(2)}, u32[]{:S(2)}) collective-permute-start(bf16[256,1024]{0,1:T(8,128)(2,1)S(1)} %bitcast.60), channel_id=1, source_target_pairs={{15,0},{16,1},{17,2},{18,3},{19,4},{20,5},{21,6},{22,7},{23,8},{24... | collective-permute-start | bytes 1572872 | tf_op jit(solution)/shard_map/ppermute | solution.py:25
  309.3 65.4 %collective-permute-start.31 = (bf16[256,1024]{0,1:T(8,128)(2,1)S(1)}, bf16[256,1024]{0,1:T(8,128)(2,1)S(1)}, u32[]{:S(2)}, u32[]{:S(2)}) collective-permute-start(bf16[256,1024]{0,1:T(8,128)(2,1)S(1)} %bitcast.61), channel_id=1, source_target_pairs={{16,0},{17,1},{18,2},{19,3},{20,4},{21,5},{22,6},{23,7},{24,8},{25... | collective-permute-start | bytes 1572872 | tf_op jit(solution)/shard_map/ppermute | solution.py:25
  374.6 15.5 %copy-start.1 = (bf16[8448,1024]{0,1:T(8,128)(2,1)}, bf16[8448,1024]{0,1:T(8,128)(2,1)S(1)}, u32[]{:S(2)}) copy-start(bf16[8448,1024]{0,1:T(8,128)(2,1)S(1)} %constant_dynamic-update-slice_fusion) | copy-start | bytes 51904516
  390.1 3.4 copy-start
  394.9 0.7 copy-start.2
  395.6 227.6 %all-gather.9.cloned.1.call-start = ((), (), s32[]{:S(2)}) async-start(), calls=%async_computation.4 | async-start | bytes 21135360 | tf_op jit(solution)/shard_map/all_gather | solution.py:15
  536.3 0.7 copy-start.3
  537.0 198.7 %all-gather.11.cloned.1.call-start = ((), (), s32[]{:S(2)}) async-start(), calls=%async_computation.5 | async-start | bytes 21135360 | tf_op jit(solution)/shard_map/all_gather | solution.py:15
  648.8 0.7 copy-start.4
  770.5 13.0 %all-to-all-start.2 = ((bf16[256,8,128]{2,0,1:T(8,128)(2,1)}), bf16[256,8,128]{2,0,1:T(8,128)(2,1)S(1)}, u32[]{:S(2)}, u32[]{:S(2)}) async-start(bf16[256,8,128]{2,0,1:T(8,128)(2,1)} %bitcast.27), calls=%async_computation.2 | async-start | bytes 1048576 | tf_op jit(solution)/shard_map/all_to_all | solution.py:106
Sparse Core Ops, SparseCore 0:
  395.8 115.0 all-gather.6
  537.1 86.1 all-gather.8
  649.6 86.1 all-gather.10
